TPU v7x, 32 devices: a whole 2x2x4 slice. The times are simulated.
32 devices in a mesh: groups: 2 (over y), tm: 4 (over z), comp: 2 (over core), panel: 2 (over x).
Axes of the slice: x: 2, y: 2, z: 4, core: 2. Of those that a mesh axis runs over, the one named last changes fastest.
Arguments:
- orbit_angles: float32 [2, 8192], P(None, ('groups', 'tm')), parts along dimension 1, may hold values from -3.15 to 3.15, as said below
- gap_mask: int32 [8192], P(('groups', 'tm')), parts along dimension 0, may hold values 0 or 1
- column_index: int32 [2, 512], P(None, 'panel'), may hold values from -280 to 280, as said below
- lat_coeffs: bfloat16 [2, 640, 512], P('comp', None, 'panel'), may hold values from -6 to 6
- psd_table: int32 [2, 2049], P('comp'), may hold values from 1024 to 32752, as said below
Outputs:
- normals: float32 [1024, 512], P(('groups', 'tm'), 'panel'), parts along dimension 0
There are 2 independent parts, one for each index of `groups`. A program takes and returns all parts, laid end to end along the dimension named above; an argument that names none is the same for every part. Nothing has to cross between parts.
Inputs may be any that keep to these rules, and one draw needn't show every extreme that they name: orbit_angles holds colatitude in its first row and longitude in its second. `column_index`: the first row holds each unknown's degree, the second its order; a degree is at least 2 and at least the order's magnitude; a negative order stands for the sine term in longitude. `psd_table`: entry g of a component's row is its noise power at frequency g (and 4096 - g), times 8192.
All inputs are finite; a program needn't handle non-finite values. No bound on the sum of `gap_mask` on one device may be relied on, other than what follows from the above.
Results may differ from a plain program's by a relative error of at most 0.0016.
Values may be sent and summed in bfloat16 or wider, within the bound.
No kernel may reach another device: no remote copies, remote signals or barrier semaphores. Data moves between devices by JAX's collectives and lax.ppermute only.
A program may use at most 64 MiB of HBM per device.

v0:
```python
import math
import jax
import jax.numpy as jnp
from jax import lax
from jax.sharding import PartitionSpec as P

SPLIT = 64


def synthesize(angles, keep_rows, column_index, coeffs):
    terms_lat = coeffs.shape[0] // 2
    colatitude = angles[0]
    longit = angles[1]
    wavenumbers = jnp.arange(terms_lat, dtype=jnp.float32)
    phases = colatitude[:, None] * wavenumbers[None, :]
    basis_rows = jnp.concatenate([jnp.cos(phases), jnp.sin(phases)], axis=1).astype(jnp.bfloat16)
    degree = column_index[0]
    orders = column_index[1]
    levels = jnp.arange(2 * terms_lat, dtype=jnp.int32) % terms_lat
    allowed = levels[:, None] <= degree[None, :]
    masked = jnp.where(allowed, coeffs, jnp.zeros_like(coeffs))
    latitude = jnp.dot(basis_rows, masked, preferred_element_type=jnp.float32)
    lon_phase = longit[:, None] * jnp.abs(orders).astype(jnp.float32)[None, :]
    lon_wave = jnp.where(orders[None, :] >= 0, jnp.cos(lon_phase), jnp.sin(lon_phase))
    norm_scale = 1.0 / jnp.sqrt(degree.astype(jnp.float32) + 1.0)
    return latitude * lon_wave * (keep_rows[:, None] * norm_scale[None, :])


def phase_tables(row_index, col_index, length):
    product = row_index[:, None] * col_index[None, :] % length
    angle_grid = product.astype(jnp.float32) * (2.0 * math.pi / length)
    return (jnp.cos(angle_grid), jnp.sin(angle_grid))


def dft_tables(length):
    indices = jnp.arange(length, dtype=jnp.int32)
    return phase_tables(indices, indices, length)


def rotate(real_part, imag_part, outer_index, inner_index, length):
    index_grid = outer_index[:, None] * inner_index[None, :] % length
    angle_grid = index_grid.astype(jnp.float32) * (2.0 * math.pi / length)
    cosine = jnp.cos(angle_grid)[:, :, None]
    sine_grid = jnp.sin(angle_grid)[:, :, None]
    return (real_part * cosine + imag_part * sine_grid, imag_part * cosine - real_part * sine_grid)


def precise_dot(left_side, right_side):
    return jnp.dot(
        left_side, right_side, precision=lax.Precision.HIGHEST, preferred_element_type=jnp.float32
    )


def transform(cos_table, sin_table, real_part, imag_part):
    new_real = precise_dot(cos_table, real_part) + precise_dot(sin_table, imag_part)
    new_imag = precise_dot(cos_table, imag_part) - precise_dot(sin_table, real_part)
    return (new_real, new_imag)


def four_step(real_in, imag_in, samples):
    length = real_in.shape[0]
    columns = real_in.shape[1]
    outer_count = SPLIT
    inner_count = length // SPLIT
    real_part = real_in.reshape(outer_count, inner_count * columns)
    imag_part = imag_in.reshape(outer_count, inner_count * columns)
    cos_outer, sin_outer = dft_tables(outer_count)
    real_part, imag_part = transform(cos_outer, sin_outer, real_part, imag_part)
    real_part = real_part.reshape(outer_count, inner_count, columns)
    imag_part = imag_part.reshape(outer_count, inner_count, columns)
    real_part, imag_part = rotate(
        real_part,
        imag_part,
        jnp.arange(outer_count, dtype=jnp.int32),
        jnp.arange(inner_count, dtype=jnp.int32),
        length,
    )
    real_part = jnp.transpose(real_part, (1, 0, 2)).reshape(inner_count, outer_count * columns)
    imag_part = jnp.transpose(imag_part, (1, 0, 2)).reshape(inner_count, outer_count * columns)
    cos_inner, sin_inner = dft_tables(inner_count)
    real_part, imag_part = transform(cos_inner, sin_inner, real_part, imag_part)
    return (
        real_part.reshape(length, columns) / samples,
        imag_part.reshape(length, columns) / samples,
    )


def local_transform(received, samples):
    real_part, imag_part = four_step(received[0, 0], received[1, 0], samples)
    return (real_part.astype(jnp.bfloat16), imag_part.astype(jnp.bfloat16))


def noise_weighted(spectra, psd_row, frequency, samples):
    folded = jnp.minimum(frequency, samples - frequency)
    inverse_psd = 8192.0 / jnp.take(psd_row, folded).astype(jnp.float32)
    return (spectra.astype(jnp.float32) * inverse_psd[None, :, None]).astype(jnp.bfloat16)


def settle(partial_value, sum_dim):
    summed = lax.psum_scatter(partial_value, "tm", scatter_dimension=sum_dim, tiled=True)
    return lax.psum(summed, "comp")


def body(orbit_angles, gap_mask, column_index, lat_coeffs, psd_table):
    devices_tm = lax.axis_size("tm")
    epochs = orbit_angles.shape[1]
    block_len = epochs // devices_tm
    samples = epochs * devices_tm
    columns = lat_coeffs.shape[2]
    coeffs = lat_coeffs[0]
    keep_rows = gap_mask.astype(jnp.float32)
    packed = jnp.concatenate([orbit_angles, keep_rows[None]], axis=0)[:, None, :]
    received = lax.all_to_all(packed, "tm", split_axis=2, concat_axis=1, tiled=True)
    flat_orbit = received.reshape(3, devices_tm * block_len)
    spread = synthesize(flat_orbit[0:2], flat_orbit[2], column_index, coeffs).reshape(
        devices_tm, block_len, columns
    )
    position = lax.axis_index("tm")
    local_epoch = position * block_len + jnp.arange(block_len, dtype=jnp.int32)
    cos_outer, sin_outer = dft_tables(devices_tm)
    flat_design = spread.reshape(devices_tm, block_len * columns)
    real_part = precise_dot(cos_outer, flat_design).reshape(devices_tm, block_len, columns)
    imag_part = -precise_dot(sin_outer, flat_design).reshape(devices_tm, block_len, columns)
    real_part, imag_part = rotate(
        real_part, imag_part, jnp.arange(devices_tm, dtype=jnp.int32), local_epoch, samples
    )
    twisted = jnp.stack([real_part, imag_part])
    spec_real, spec_imag = local_transform(
        lax.all_to_all(twisted, "tm", split_axis=1, concat_axis=2, tiled=True), samples
    )
    spectra = jnp.stack([spec_real, spec_imag])
    psd_row = psd_table[0]
    contract = (((0, 1), (0, 1)), ((), ()))
    frequency = position + devices_tm * jnp.arange(epochs, dtype=jnp.int32)
    weighted = noise_weighted(spectra, psd_row, frequency, samples)
    partial_value = lax.dot_general(
        lax.all_gather(spectra, "panel", axis=2, tiled=True),
        weighted,
        contract,
        preferred_element_type=jnp.float32,
    )
    return settle(partial_value, 0)


def solution(mesh):
    return jax.shard_map(
        body,
        mesh=mesh,
        in_specs=(
            P(None, ("groups", "tm")),
            P(("groups", "tm")),
            P(None, "panel"),
            P("comp", None, "panel"),
            P("comp", None),
        ),
        out_specs=P(("groups", "tm"), "panel"),
        check_vma=False,
    )
```

profile of v0, /device:TPU:0, one launch (start us, length us, event | category | flops | bytes accessed | tf_op | source)
XLA Modules:
  0.0 205.0 jit_solution(10367188866137886708)
XLA Ops:
  6.5 0.7 convert_element_type.103
  7.3 0.7 pad_maximum_fusion.2
  8.0 0.2 copy.46
  8.2 0.6 broadcast.344
  8.8 2.0 reduce.9
  10.8 1.0 reshape.246
  11.8 6.4 %all-to-all-start = ((f32[4,1,768]{2,1,0:T(1,128)}), f32[4,1,768]{2,1,0:T(1,128)S(1)}, u32[]{:S(2)}, u32[]{:S(2)}) async-start(f32[4,1,768]{2,1,0:T(1,128)} %reshape.246), calls=%async_computation | async-start | bytes 24576 | tf_op jit(solution)/shard_map/all_to_all | solution.py:113
  18.4 0.1 copy.47
  18.5 0.1 copy.48
  18.7 5.2 %all-to-all-done = f32[4,1,768]{2,1,0:T(1,128)S(1)} async-done(((f32[4,1,768]{2,1,0:T(1,128)}), f32[4,1,768]{2,1,0:T(1,128)S(1)}, u32[]{:S(2)}, u32[]{:S(2)}) %all-to-all-start) | async-done | bytes 12320 | tf_op jit(solution)/shard_map/all_to_all | solution.py:113
  23.8 0.7 reduce.10
  24.6 0.7 reshape.247
  25.3 10.4 %slice_reduce_fusion.1 = (f32[1024]{0:T(1024)S(1)}, f32[1024]{0:T(1024)S(1)}, f32[1024]{0:T(1024)S(1)}) fusion(f32[3,1,1024]{0,1,2:T(1,128)S(1)} %bitcast.77), kind=kLoop, calls=%fused_computation.36 | loop fusion | bytes 24576 | tf_op jit(solution)/shard_map/slice | solution.py:13
  35.7 6.5 %cosine_convert_fusion = (bf16[1024,320]{1,0:T(8,128)(2,1)S(1)}, bf16[1024,320]{1,0:T(8,128)(2,1)S(1)}) fusion(f32[1024]{0:T(1024)S(1)} %get-tuple-element.7), kind=kLoop, calls=%fused_computation.12 | loop fusion | flops 983040 | bytes 1314816 | tf_op jit(solution)/shard_map/convert
  42.3 4.4 %fusion.4 = f32[1024,256]{1,0:T(8,128)S(1)} fusion(bf16[1024,320]{1,0:T(8,128)(2,1)S(1)} %get-tuple-element.15, bf16[1024,320]{1,0:T(8,128)(2,1)S(1)} %get-tuple-element.14, f32[256]{0:T(256)S(1)} %bitcast.85, f32[1024]{0:T(1024)S(1)} %get-tuple-element.6, f32[256]{0:T(256)S(1)} %bitcast.87, f32[1024]{0:T(1024)S(1)} %get-tuple-element.5, ...), kind=kOutput, calls=%fused_computation.18 | convolution fusion | flops 339804160 | bytes 2701056 | tf_op jit(solution)/shard_map/dot_general | solution.py:22
  46.7 0.5 reshape_reshape.3
  47.2 1.9 convolution_negate_fusion
  49.2 2.8 %add_bitcast_fusion = (f32[1,4,256,256]{3,1,2,0:T(4,128)S(1)}, f32[1,4,256,256]{3,1,2,0:T(4,128)S(1)}) fusion(f32[4,256,256]{2,0,1:T(4,128)S(1)} %convolution_negate_fusion, f32[4,256]{0,1:T(8,128)S(1)} %copy.48, f32[4,256]{0,1:T(8,128)S(1)} %copy.47, f32[256,256,4]{1,2,0:T(4,128)S(1)} %bitcast.72), kind=kOutput, calls=%fused_computation.33 | convolution fusion | flops 14156000 | bytes 4202496 | tf_op jit(solution)/shard_map/dot_general | solution.py:49
  52.0 0.5 pad_maximum_fusion
  52.4 1.7 copy.49
  54.2 3.6 %all-to-all-start.1 = ((f32[2,4,256,256]{3,2,0,1:T(8,128)}), f32[2,4,256,256]{3,2,0,1:T(8,128)S(1)}, u32[]{:S(2)}, u32[]{:S(2)}) async-start(f32[2,4,256,256]{3,2,0,1:T(8,128)} %copy.49), calls=%async_computation.1 | async-start | bytes 4194304 | tf_op jit(solution)/shard_map/all_to_all | solution.py:129
  57.8 0.3 all-gather.2.cloned.1.call-start
  58.1 46.7 %all-to-all-done.1 = f32[2,4,256,256]{3,2,0,1:T(8,128)S(1)} async-done(((f32[2,4,256,256]{3,2,0,1:T(8,128)}), f32[2,4,256,256]{3,2,0,1:T(8,128)S(1)}, u32[]{:S(2)}, u32[]{:S(2)}) %all-to-all-start.1) | async-done | bytes 2097184 | tf_op jit(solution)/shard_map/all_to_all | solution.py:129
  104.8 1.1 fusion.115
  105.9 0.2 reshape_squeeze.6
  106.1 1.2 fusion.26
  107.3 1.4 reshape_squeeze.7
  108.7 1.2 fusion.24
  109.9 1.2 convolution_add_fusion.1
  111.1 1.2 convolution_subtract_fusion.1
  112.3 0.3 fusion.9
  112.6 0.6 copy.60
  113.3 1.0 fusion.55
  114.3 0.6 copy.61
  114.9 1.0 fusion.53
  116.0 1.1 fusion.2
  117.1 0.2 convert_element_type.109
  117.3 1.0 copy.54
  118.3 1.1 fusion.3
  119.5 0.2 convert_element_type.111
  119.7 0.2 copy.55
  119.9 1.1 pad_maximum_fusion.1
  121.2 6.2 %gather_fusion = s32[1024]{0:T(1024)S(1)} fusion(s32[2049]{0:T(1024)S(1)} %reduce.4, s32[1024]{0:T(1024)S(1)} %broadcast_clamp_fusion), kind=kCustom, calls=%fused_computation | custom fusion | bytes 12288 | tf_op jit(solution)/shard_map/jit(_take)/gather | solution.py:95
  127.3 26.1 %all-gather.2.cloned.1.call-done = bf16[2,1024,512]{1,2,0:T(8,128)(2,1)} async-done(((bf16[2,1024,256]{1,2,0:T(8,128)(2,1)}), bf16[2,1024,512]{1,2,0:T(8,128)(2,1)}) %all-gather.2.cloned.1.call-update) | async-done | bytes 2097168 | tf_op jit(solution)/shard_map/all_gather | solution.py:137
  153.4 3.1 %convolution_bitcast_fusion = f32[512,256]{1,0:T(8,128)} fusion(bf16[2,1024,512]{1,2,0:T(8,128)(2,1)} %all-gather.2.cloned.1.call-done, f32[1024]{0:T(1024)S(1)} %convert_divide_fusion, bf16[1,1024,256]{1,2,0:T(8,128)(2,1)S(1)} %copy.55, bf16[1,1024,256]{1,2,0:T(8,128)(2,1)S(1)} %copy-done.1), kind=kOutput, calls=%fused_computation.22 | convolution fusion | flops 538968064 | bytes 3674112 | tf_op jit(solution)/shard_map/dot_general | solution.py:136
  156.6 21.8 %reduce-scatter.2.cloned.1.call-done = f32[128,256]{1,0:T(8,128)} async-done(((f32[512,256]{1,0:T(8,128)}), f32[128,256]{1,0:T(8,128)}) %reduce-scatter.2.cloned.1.call-update) | async-done | bytes 131088 | tf_op jit(solution)/shard_map/reduce_scatter | solution.py:100
  178.4 18.5 %all-reduce.2.cloned.1.call-done = f32[128,256]{1,0:T(8,128)} async-done(((f32[128,256]{1,0:T(8,128)}), f32[128,256]{1,0:T(8,128)}) %all-reduce.2.cloned.1.call-update) | async-done | bytes 131088 | tf_op jit(solution)/shard_map/psum | solution.py:101
  196.9 1.6 copy.67
  (24 shorter events, 0.4 us)
Async XLA Ops:
  6.5 114.5 %copy-start = (s32[1,2049]{1,0:T(1,128)S(1)}, s32[1,2049]{1,0:T(1,128)}, u32[]{:S(2)}) copy-start(s32[1,2049]{1,0:T(1,128)} %param.9) | copy-start | bytes 24592
  6.5 11.7 %copy-start.2 = (s32[2,256]{1,0:T(2,128)S(1)}, s32[2,256]{1,0:T(2,128)}, u32[]{:S(2)}) copy-start(s32[2,256]{1,0:T(2,128)} %param.7) | copy-start | bytes 6148
  11.8 30.5 %copy-start.3 = (bf16[1,640,256]{2,1,0:T(8,128)(2,1)S(1)}, bf16[1,640,256]{2,1,0:T(8,128)(2,1)}, u32[]{:S(2)}) copy-start(bf16[1,640,256]{2,1,0:T(8,128)(2,1)} %param.8) | copy-start | bytes 983044
  11.8 12.1 %all-to-all-start = ((f32[4,1,768]{2,1,0:T(1,128)}), f32[4,1,768]{2,1,0:T(1,128)S(1)}, u32[]{:S(2)}, u32[]{:S(2)}) async-start(f32[4,1,768]{2,1,0:T(1,128)} %reshape.246), calls=%async_computation | async-start | bytes 24576 | tf_op jit(solution)/shard_map/all_to_all | solution.py:113
  54.2 50.6 %all-to-all-start.1 = ((f32[2,4,256,256]{3,2,0,1:T(8,128)}), f32[2,4,256,256]{3,2,0,1:T(8,128)S(1)}, u32[]{:S(2)}, u32[]{:S(2)}) async-start(f32[2,4,256,256]{3,2,0,1:T(8,128)} %copy.49), calls=%async_computation.1 | async-start | bytes 4194304 | tf_op jit(solution)/shard_map/all_to_all | solution.py:129
  57.8 95.6 %all-gather.2.cloned.1.call-start = ((), (), s32[]{:S(2)}) async-start(), calls=%async_computation.3 | async-start | bytes 3145728 | tf_op jit(solution)/shard_map/all_gather | solution.py:137
  118.3 1.6 copy-start.1
  121.0 57.4 %reduce-scatter.2.cloned.1.call-start = ((), (), s32[]{:S(2)}) async-start(), calls=%async_computation.4 | async-start | bytes 655360 | tf_op jit(solution)/shard_map/reduce_scatter | solution.py:100
  156.6 40.3 %all-reduce.2.cloned.1.call-start = ((), (), s32[]{:S(2)}) async-start(), calls=%async_computation.5 | async-start | bytes 262144 | tf_op jit(solution)/shard_map/psum | solution.py:101
Sparse Core Ops, SparseCore 0:
  121.1 32.2 all-gather.1
  156.7 21.6 reduce-scatter.1
  180.7 16.1 all-reduce.1
where the time goes:
time: 205 us
  waiting for transfers between devices  118 us (58%)
  local copies, waits for them, and re-layouts  28.8 us (14%)
  matrix products  21.3 us (10%)
  between operations  13.4 us (7%)
  other arithmetic  12.8 us (6%)
  starting transfers between devices  10.4 us (5%)
    all_to_all x1, waiting for transfers between devices, body(): lax.all_to_all(twisted, 'tm', split_axis=1, concat_axis=2, tiled=True)  46.7 us
    all_gather x1, waiting for transfers between devices, body(): lax.all_gather(spectra, 'panel', axis=2, tiled=True)  26.1 us
    reduce_scatter x1, waiting for transfers between devices, settle(): lax.psum_scatter(partial_value, 'tm', scatter_dimension=sum_dim, tiled=True)  21.8 us
    psum x1, waiting for transfers between devices, settle(): return lax.psum(summed, 'comp')  18.5 us
    dot_general x10, matrix products, precise_dot(): jnp.dot(left_side, right_side, precision=lax.Precision.HIGHEST, preferred...  13.8 us
    slice x1, local copies, waits for them, and re-layouts, synthesize(): longit = angles[1]  10.4 us
    another operation x1, other arithmetic  6.55 us
    all_to_all x1, starting transfers between devices, body(): lax.all_to_all(packed, 'tm', split_axis=2, concat_axis=1, tiled=True)  6.45 us
  transfers between devices with their start and end apart: 5, of which 5 were waited for; matrix products, arithmetic and copies ran while one was open for 3% of the time, Pallas kernels for 0%

commit v1 on v0

--- a/solution.py
+++ b/solution.py
@@ -98,7 +98,7 @@
 
 def settle(partial_value, sum_dim):
     summed = lax.psum_scatter(partial_value, "tm", scatter_dimension=sum_dim, tiled=True)
-    return lax.psum(summed, "comp")
+    return jnp.sum(lax.all_gather(summed, "comp"), 0)
 
 
 def body(orbit_angles, gap_mask, column_index, lat_coeffs, psd_table):

time: 205 us -> 189 us (0.922)
  waiting for transfers between devices: 118 us -> 99.8 us
  blocking collectives: 0 us -> 2.19 us
    psum x1 -> x0, waiting for transfers between devices: 18.5 us -> none  [settle(): return lax.psum(summed, 'comp')]
    all_gather x0 -> x1, blocking collectives: none -> 2.19 us  [settle(): return jnp.sum(lax.all_gather(summed, 'comp'), 0)]
    unnamed x14 -> x13, local copies, waits for them, and re-layouts: 5.05 us -> 3.49 us
  transfers between devices with their start and end apart: 5 -> 4, of which waited for: 5 -> 4; matrix products, arithmetic and copies ran while one was open for 3% -> 4% of each run, Pallas kernels for 0% -> 0%
where the time goes in v1:
time: 189 us; the launch traced here: 188 us
  waiting for transfers between devices  99.8 us (53%)
  local copies, waits for them, and re-layouts  27.3 us (14%)
  matrix products  21.3 us (11%)
  between operations  13.7 us (7%)
  other arithmetic  13.5 us (7%)
  starting transfers between devices  10.4 us (6%)
  blocking collectives  2.19 us (1%)
    all_to_all x1, waiting for transfers between devices, body(): lax.all_to_all(twisted, 'tm', split_axis=1, concat_axis=2, tiled=True)  46.7 us
    all_gather x1, waiting for transfers between devices, body(): lax.all_gather(spectra, 'panel', axis=2, tiled=True)  26.1 us
    reduce_scatter x1, waiting for transfers between devices, settle(): lax.psum_scatter(partial_value, 'tm', scatter_dimension=sum_dim, tiled=True)  21.8 us
    dot_general x10, matrix products, precise_dot(): jnp.dot(left_side, right_side, precision=lax.Precision.HIGHEST, preferred...  13.8 us
    slice x1, local copies, waits for them, and re-layouts, synthesize(): longit = angles[1]  10.4 us
    another operation x1, other arithmetic  6.55 us
    all_to_all x1, starting transfers between devices, body(): lax.all_to_all(packed, 'tm', split_axis=2, concat_axis=1, tiled=True)  6.45 us
    gather x1, local copies, waits for them, and re-layouts, noise_weighted(): inverse_psd = 8192.0 / jnp.take(psd_row, folded).astype(jnp.float32)  6.15 us
  transfers between devices with their start and end apart: 4, of which 4 were waited for; matrix products, arithmetic and copies ran while one was open for 4% of the time, Pallas kernels for 0%

profile of v1, /device:TPU:0, one launch (start us, length us, event | category | flops | bytes accessed | tf_op | source)
XLA Modules:
  0.0 188.1 jit_solution(5268075955193681397)
XLA Ops:
  6.5 0.7 convert_element_type.103
  7.3 0.7 pad_maximum_fusion.2
  8.0 0.2 copy.46
  8.2 0.6 broadcast.344
  8.8 2.0 %reduce.9 = f32[1024,3]{1,0:T(8,128)S(1)} reduce(f32[1024,1,3]{2,1,0:T(1,128)S(1)} %bitcast.83, f32[]{:T(128)} %broadcast.344), dimensions={1}, to_apply=%bitcast.57.reduce_sub_computation | reduce | bytes 24580
  10.8 1.0 reshape.247
  11.8 6.4 %all-to-all-start = ((f32[4,1,768]{2,1,0:T(1,128)}), f32[4,1,768]{2,1,0:T(1,128)S(1)}, u32[]{:S(2)}, u32[]{:S(2)}) async-start(f32[4,1,768]{2,1,0:T(1,128)} %reshape.247), calls=%async_computation | async-start | bytes 24576 | tf_op jit(solution)/shard_map/all_to_all | solution.py:113
  18.4 0.1 copy.47
  18.5 0.1 copy.48
  18.7 5.2 %all-to-all-done = f32[4,1,768]{2,1,0:T(1,128)S(1)} async-done(((f32[4,1,768]{2,1,0:T(1,128)}), f32[4,1,768]{2,1,0:T(1,128)S(1)}, u32[]{:S(2)}, u32[]{:S(2)}) %all-to-all-start) | async-done | bytes 12320 | tf_op jit(solution)/shard_map/all_to_all | solution.py:113
  23.8 0.7 reduce.10
  24.6 0.7 reshape.248
  25.3 10.4 %slice_reduce_fusion.1 = (f32[1024]{0:T(1024)S(1)}, f32[1024]{0:T(1024)S(1)}, f32[1024]{0:T(1024)S(1)}) fusion(f32[3,1,1024]{0,1,2:T(1,128)S(1)} %bitcast.78), kind=kLoop, calls=%fused_computation.36 | loop fusion | bytes 24576 | tf_op jit(solution)/shard_map/slice | solution.py:13
  35.7 6.5 %cosine_convert_fusion = (bf16[1024,320]{1,0:T(8,128)(2,1)S(1)}, bf16[1024,320]{1,0:T(8,128)(2,1)S(1)}) fusion(f32[1024]{0:T(1024)S(1)} %get-tuple-element.7), kind=kLoop, calls=%fused_computation.12 | loop fusion | flops 983040 | bytes 1314816 | tf_op jit(solution)/shard_map/convert
  42.3 4.4 %fusion.4 = f32[1024,256]{1,0:T(8,128)S(1)} fusion(bf16[1024,320]{1,0:T(8,128)(2,1)S(1)} %get-tuple-element.15, bf16[1024,320]{1,0:T(8,128)(2,1)S(1)} %get-tuple-element.14, f32[256]{0:T(256)S(1)} %bitcast.87, f32[1024]{0:T(1024)S(1)} %get-tuple-element.6, f32[256]{0:T(256)S(1)} %bitcast.89, f32[1024]{0:T(1024)S(1)} %get-tuple-element.5, ...), kind=kOutput, calls=%fused_computation.18 | convolution fusion | flops 339804160 | bytes 2701056 | tf_op jit(solution)/shard_map/dot_general | solution.py:22
  46.7 0.5 reshape_reshape.3
  47.2 1.9 %convolution_negate_fusion = f32[4,256,256]{2,0,1:T(4,128)S(1)} fusion(f32[256,256,4]{1,2,0:T(4,128)S(1)} %bitcast.72), kind=kOutput, calls=%fused_computation.16 | convolution fusion | flops 12845280 | bytes 2097152 | tf_op jit(solution)/shard_map/dot_general | solution.py:49
  49.2 2.8 %add_bitcast_fusion = (f32[1,4,256,256]{3,1,2,0:T(4,128)S(1)}, f32[1,4,256,256]{3,1,2,0:T(4,128)S(1)}) fusion(f32[4,256,256]{2,0,1:T(4,128)S(1)} %convolution_negate_fusion, f32[4,256]{0,1:T(8,128)S(1)} %copy.48, f32[4,256]{0,1:T(8,128)S(1)} %copy.47, f32[256,256,4]{1,2,0:T(4,128)S(1)} %bitcast.73), kind=kOutput, calls=%fused_computation.33 | convolution fusion | flops 14156000 | bytes 4202496 | tf_op jit(solution)/shard_map/dot_general | solution.py:49
  52.0 0.5 pad_maximum_fusion
  52.4 1.7 copy.49
  54.2 3.6 %all-to-all-start.1 = ((f32[2,4,256,256]{3,2,0,1:T(8,128)}), f32[2,4,256,256]{3,2,0,1:T(8,128)S(1)}, u32[]{:S(2)}, u32[]{:S(2)}) async-start(f32[2,4,256,256]{3,2,0,1:T(8,128)} %copy.49), calls=%async_computation.1 | async-start | bytes 4194304 | tf_op jit(solution)/shard_map/all_to_all | solution.py:129
  57.8 0.3 all-gather.3.cloned.1.call-start
  58.1 46.7 %all-to-all-done.1 = f32[2,4,256,256]{3,2,0,1:T(8,128)S(1)} async-done(((f32[2,4,256,256]{3,2,0,1:T(8,128)}), f32[2,4,256,256]{3,2,0,1:T(8,128)S(1)}, u32[]{:S(2)}, u32[]{:S(2)}) %all-to-all-start.1) | async-done | bytes 2097184 | tf_op jit(solution)/shard_map/all_to_all | solution.py:129
  104.8 1.1 fusion.115
  105.9 0.2 reshape_squeeze.6
  106.1 1.2 fusion.26
  107.3 1.4 reshape_squeeze.7
  108.7 1.2 fusion.24
  109.9 1.2 convolution_add_fusion.1
  111.1 1.2 convolution_subtract_fusion.1
  112.3 0.3 fusion.9
  112.6 0.6 copy.60
  113.3 1.0 fusion.55
  114.3 0.6 copy.61
  114.9 1.0 fusion.53
  116.0 1.1 fusion.2
  117.1 0.2 convert_element_type.109
  117.3 1.0 copy.54
  118.3 1.1 fusion.3
  119.5 0.2 convert_element_type.111
  119.7 0.2 copy.55
  119.9 1.1 pad_maximum_fusion.1
  121.2 6.2 %gather_fusion = s32[1024]{0:T(1024)S(1)} fusion(s32[2049]{0:T(1024)S(1)} %reduce.4, s32[1024]{0:T(1024)S(1)} %broadcast_clamp_fusion), kind=kCustom, calls=%fused_computation | custom fusion | bytes 12288 | tf_op jit(solution)/shard_map/jit(_take)/gather | solution.py:95
  127.3 26.1 %all-gather.3.cloned.1.call-done = bf16[2,1024,512]{1,2,0:T(8,128)(2,1)} async-done(((bf16[2,1024,256]{1,2,0:T(8,128)(2,1)}), bf16[2,1024,512]{1,2,0:T(8,128)(2,1)}) %all-gather.3.cloned.1.call-update) | async-done | bytes 2097168 | tf_op jit(solution)/shard_map/all_gather | solution.py:137
  153.4 3.1 %convolution_bitcast_fusion = f32[512,256]{1,0:T(8,128)} fusion(bf16[2,1024,512]{1,2,0:T(8,128)(2,1)} %all-gather.3.cloned.1.call-done, f32[1024]{0:T(1024)S(1)} %convert_divide_fusion, bf16[1,1024,256]{1,2,0:T(8,128)(2,1)S(1)} %copy.55, bf16[1,1024,256]{1,2,0:T(8,128)(2,1)S(1)} %copy-done.1), kind=kOutput, calls=%fused_computation.22 | convolution fusion | flops 538968064 | bytes 3674112 | tf_op jit(solution)/shard_map/dot_general | solution.py:136
  156.6 21.8 %reduce-scatter.2.cloned.1.call-done = f32[128,256]{1,0:T(8,128)} async-done(((f32[512,256]{1,0:T(8,128)}), f32[128,256]{1,0:T(8,128)}) %reduce-scatter.2.cloned.1.call-update) | async-done | bytes 131088 | tf_op jit(solution)/shard_map/reduce_scatter | solution.py:100
  178.4 2.2 %all-gather = f32[256,256]{1,0:T(8,128)S(1)} all-gather(f32[128,256]{1,0:T(8,128)} %reduce-scatter.2.cloned.1.call-done), channel_id=2, replica_groups=mesh['groups'=2,'tm'=4,'comp'=2,'panel'=2] {'comp'}, dimensions={0}, use_global_device_ids=true | all-gather | bytes 393216 | tf_op jit(solution)/shard_map/all_gather | solution.py:101
  180.6 0.7 reduce_sum.9
  (22 shorter events, 0.3 us)
Async XLA Ops:
  6.5 114.5 %copy-start = (s32[1,2049]{1,0:T(1,128)S(1)}, s32[1,2049]{1,0:T(1,128)}, u32[]{:S(2)}) copy-start(s32[1,2049]{1,0:T(1,128)} %param.9) | copy-start | bytes 24592
  6.5 11.7 %copy-start.2 = (s32[2,256]{1,0:T(2,128)S(1)}, s32[2,256]{1,0:T(2,128)}, u32[]{:S(2)}) copy-start(s32[2,256]{1,0:T(2,128)} %param.7) | copy-start | bytes 6148
  11.8 30.5 %copy-start.3 = (bf16[1,640,256]{2,1,0:T(8,128)(2,1)S(1)}, bf16[1,640,256]{2,1,0:T(8,128)(2,1)}, u32[]{:S(2)}) copy-start(bf16[1,640,256]{2,1,0:T(8,128)(2,1)} %param.8) | copy-start | bytes 983044
  11.8 12.1 %all-to-all-start = ((f32[4,1,768]{2,1,0:T(1,128)}), f32[4,1,768]{2,1,0:T(1,128)S(1)}, u32[]{:S(2)}, u32[]{:S(2)}) async-start(f32[4,1,768]{2,1,0:T(1,128)} %reshape.247), calls=%async_computation | async-start | bytes 24576 | tf_op jit(solution)/shard_map/all_to_all | solution.py:113
  54.2 50.6 %all-to-all-start.1 = ((f32[2,4,256,256]{3,2,0,1:T(8,128)}), f32[2,4,256,256]{3,2,0,1:T(8,128)S(1)}, u32[]{:S(2)}, u32[]{:S(2)}) async-start(f32[2,4,256,256]{3,2,0,1:T(8,128)} %copy.49), calls=%async_computation.1 | async-start | bytes 4194304 | tf_op jit(solution)/shard_map/all_to_all | solution.py:129
  57.8 95.6 %all-gather.3.cloned.1.call-start = ((), (), s32[]{:S(2)}) async-start(), calls=%async_computation.3 | async-start | bytes 3145728 | tf_op jit(solution)/shard_map/all_gather | solution.py:137
  118.3 1.6 copy-start.1
  121.0 57.4 %reduce-scatter.2.cloned.1.call-start = ((), (), s32[]{:S(2)}) async-start(), calls=%async_computation.4 | async-start | bytes 655360 | tf_op jit(solution)/shard_map/reduce_scatter | solution.py:100
Sparse Core Ops, SparseCore 0:
  121.1 32.2 all-gather.2
  156.7 21.6 reduce-scatter.1
